TPU v7x, 32 devices: a whole 2x2x4 slice. The times are simulated.
32 devices in a mesh: date: 16 (over z, x, core), strip: 2 (over y).
Axes of the slice: x: 2, y: 2, z: 4, core: 2. Of those that a mesh axis runs over, the one named last changes fastest.
Arguments:
- slc: bfloat16 [128, 2, 512, 384], P('date', None, 'strip'), as said below
- offsets: int32 [128, 3], P('date'), may hold values from 1 to 3
- owner: int32 [16], replicated, may hold values from 0 to 15, each once
Outputs:
- interferograms: float32 [128, 3, 2, 32, 96], P('date', None, None, 'strip')
- coherence: float32 [128, 3, 32, 96], P('date', None, 'strip')
- network_mean: float32 [16, 2, 32, 6], P('date', None, 'strip')
Inputs may be any that keep to these rules, and one draw needn't show every extreme that they name: `slc`: each image is a common scene turned by a phase of its date plus noise of its date.
All inputs are finite; a program needn't handle non-finite values.
Results may differ from a plain program's by a relative error of at most 0.0003.
Values may be sent and summed in bfloat16 or wider, within the bound.
No kernel may reach another device: no remote copies, remote signals or barrier semaphores. Data moves between devices by JAX's collectives and lax.ppermute only.
A program may use at most 128 MiB of HBM per device.

v0:
```python
import jax
import jax.numpy as jnp
from jax import lax
from jax.sharding import PartitionSpec as P

NB = 3
LR = 16
LA = 4


def shifted(value, axis, steps):
    count = lax.axis_size(axis)
    pairs = [(source, (source + steps) % count) for source in range(count)]
    return lax.ppermute(value, axis, pairs)


def pooling(cols):
    lines = jnp.arange(cols, dtype=jnp.int32)
    cells = jnp.arange(cols // LA, dtype=jnp.int32)
    return (lines[:, None] // LA == cells[None, :]).astype(jnp.float32)


def looks(field, pool):
    count, rows, cols = field.shape
    ranged = field.reshape(count, rows // LR, LR, cols).sum(2)
    pooled = jnp.einsum("nra,ab->nrb", ranged, pool, precision=lax.Precision.HIGHEST)
    return pooled * (1.0 / (LR * LA))


def pair_block(own_images, extended, block_offsets):
    count = own_images.shape[0]
    own = own_images.astype(jnp.float32)
    pool = pooling(own.shape[3])
    pairs = []
    coher = []
    for slot in range(NB):
        step_off = block_offsets[:, slot][:, None, None, None]
        chosen = extended[NB : NB + count]
        for dist in range(NB - 1, 0, -1):
            chosen = jnp.where(step_off == dist, extended[dist : dist + count], chosen)
        other = chosen.astype(jnp.float32)
        real_part = looks(own[:, 0] * other[:, 0] + own[:, 1] * other[:, 1], pool)
        imag_part = looks(own[:, 1] * other[:, 0] - own[:, 0] * other[:, 1], pool)
        power_a = looks(own[:, 0] * own[:, 0] + own[:, 1] * own[:, 1], pool)
        power_b = looks(other[:, 0] * other[:, 0] + other[:, 1] * other[:, 1], pool)
        pairs.append(jnp.stack([real_part, imag_part], 1))
        coher.append(
            jnp.sqrt(real_part * real_part + imag_part * imag_part)
            / jnp.sqrt(power_a * power_b + 1e-06)
        )
    return (jnp.stack(pairs, 1), jnp.stack(coher, 1))


def on_device(slc, offsets, owner):
    count = slc.shape[0]
    rim = shifted(slc[:NB], "date", -1)
    extended = jnp.concatenate([slc, rim], 0)
    interferograms, coherence = pair_block(slc, extended, offsets)
    weighted = jnp.concatenate([coherence[:, :, None] * interferograms, coherence[:, :, None]], 2)
    tile_count = owner.shape[0]
    rows_loc = weighted.shape[3]
    width = weighted.shape[4] // tile_count
    slots = jnp.arange(tile_count, dtype=jnp.int32)
    onehot = (owner[None, :] == slots[:, None]).astype(jnp.float32)
    flat = weighted.reshape(count * NB, 3, rows_loc, tile_count, width).transpose(3, 0, 1, 2, 4)
    slotted = jnp.einsum("st,tpcrw->spcrw", onehot, flat, precision=lax.Precision.HIGHEST)
    sums = lax.all_to_all(slotted, "date", split_axis=0, concat_axis=1, tiled=True).sum(1)
    network_mean = sums[:, :2] / (1.0 + sums[:, 2:3])
    return (interferograms, coherence, network_mean)


def solution(mesh):
    placed = (P("date", None, "strip", None), P("date", None), P())
    return jax.shard_map(
        on_device,
        mesh=mesh,
        in_specs=placed,
        out_specs=(
            P("date", None, None, "strip", None),
            P("date", None, "strip", None),
            P("date", None, "strip", None),
        ),
        check_vma=False,
    )
```

profile of v0, /device:TPU:0, one launch (start us, length us, event | category | flops | bytes accessed | tf_op | source)
XLA Modules:
  0.0 118.8 jit_solution(13078564321171893398)
XLA Ops:
  0.6 1.4 %slice.36 = bf16[3,2,256,384]{3,2,1,0:T(8,128)(2,1)S(1)} slice(bf16[8,2,256,384]{3,2,1,0:T(8,128)(2,1)} %param.3), slice={[0:3], [0:2], [0:256], [0:384]} | slice | bytes 2359296 | tf_op jit(solution)/shard_map/slice | solution.py:56
  2.0 5.5 %collective-permute-start = (bf16[3,2,256,384]{3,2,1,0:T(8,128)(2,1)S(1)}, bf16[3,2,256,384]{3,2,1,0:T(8,128)(2,1)S(1)}, u32[]{:S(2)}, u32[]{:S(2)}) collective-permute-start(bf16[3,2,256,384]{3,2,1,0:T(8,128)(2,1)S(1)} %slice.36), channel_id=1, source_target_pairs={{0,30},{2,0},{4,2},{6,4},{8,6},{10,8},{12,10},{14,12},{16,14},{18,... | collective-permute-start | bytes 3538952 | tf_op jit(solution)/shard_map/ppermute | solution.py:14
  7.5 0.8 compare_bitcast_fusion.5
  8.3 3.7 %fusion.47 = (f32[8,2,256,384]{3,2,1,0:T(8,128)S(1)}, bf16[11,2,256,384]{3,2,1,0:T(8,128)(2,1)S(1)}) fusion(bf16[8,2,256,384]{3,2,1,0:T(8,128)(2,1)} %param.3), kind=kLoop, calls=%fused_computation.82 | loop fusion | flops 1572863 | bytes 12582912 | tf_op jit(solution)/shard_map/convert_element_type | solution.py:32
  12.0 0.0 copy-start
  12.1 9.2 %collective-permute-done = bf16[3,2,256,384]{3,2,1,0:T(8,128)(2,1)S(1)} collective-permute-done((bf16[3,2,256,384]{3,2,1,0:T(8,128)(2,1)S(1)}, bf16[3,2,256,384]{3,2,1,0:T(8,128)(2,1)S(1)}, u32[]{:S(2)}, u32[]{:S(2)}) %collective-permute-start) | collective-permute-done | bytes 1179680 | tf_op jit(solution)/shard_map/ppermute | solution.py:14
  21.2 0.2 constant_dynamic-update-slice_fusion
  21.5 5.4 %select_convert_fusion.2 = (f32[8,2,256,384]{3,2,1,0:T(8,128)S(1)}, f32[8,2,256,384]{3,2,1,0:T(8,128)}, f32[8,2,256,384]{3,2,1,0:T(8,128)}) fusion(pred[8]{0:T(512)(128)(4,1)S(1)} %get-tuple-element.32, pred[8]{0:T(512)(128)(4,1)S(1)} %get-tuple-element.31, bf16[11,2,256,384]{3,2,1,0:T(8,128)(2,1)S(1)} %constant_dynamic-update-slice_fusion, ...), kind=kLoop, calls=%fused_computation.12 | loop fusion | flops 14155776 | bytes 28311600 | tf_op jit(solution)/shard_map/convert_element_type | solution.py:41
  26.9 0.0 copy-done
  26.9 4.0 %multiply_add_fusion.6 = (f32[8,1,256,384]{3,2,1,0:T(8,128)S(1)}, f32[8,1,256,384]{3,2,1,0:T(8,128)}, f32[8,1,256,384]{3,2,1,0:T(8,128)}, f32[8,1,256,384]{3,2,1,0:T(8,128)}) fusion(f32[8,2,256,384]{3,2,1,0:T(8,128)S(1)} %get-tuple-element.26, f32[8,2,256,384]{3,2,1,0:T(8,128)S(1)} %get-tuple-element.29), kind=kLoop, calls=%fused_computation.11 | loop fusion | flops 9437184 | bytes 25165824 | tf_op jit(solution)/shard_map/add | solution.py:42
  30.9 2.4 %reduce_sum.115 = f32[8,16,384]{2,1,0:T(8,128)S(1)} reduce(f32[8,16,16,384]{3,2,1,0:T(8,128)} %bitcast.97, f32[]{:T(128)} %constant.21.clone.1), dimensions={2}, to_apply=%region_6.7 | reduce | flops 737280 | bytes 3342340 | tf_op jit(solution)/shard_map/reduce_sum | solution.py:25
  33.3 3.1 %reduce_sum.110 = f32[8,16,384]{2,1,0:T(8,128)} reduce(f32[8,16,16,384]{3,2,1,0:T(8,128)} %bitcast.96, f32[]{:T(128)} %constant.21.clone.1), dimensions={2}, to_apply=%region_1.2 | reduce | flops 737280 | bytes 3342340 | tf_op jit(solution)/shard_map/reduce_sum | solution.py:25
  36.3 0.3 convolution_multiply_fusion.3
  36.6 1.2 convolution_multiply_fusion.8
  37.8 0.0 copy-start.9
  37.8 0.5 reduce_sum.109
  38.3 0.9 convolution_multiply_fusion.9
  39.2 2.5 %reduce_sum.116 = f32[8,16,384]{2,1,0:T(8,128)S(1)} reduce(f32[8,16,16,384]{3,2,1,0:T(8,128)} %bitcast.91, f32[]{:T(128)} %constant.21.clone.1), dimensions={2}, to_apply=%region_7.8 | reduce | flops 737280 | bytes 3342340 | tf_op jit(solution)/shard_map/reduce_sum | solution.py:25
  41.7 0.0 slice-start.1
  41.7 5.0 %multiply_add_fusion = f32[8,1,256,384]{3,2,1,0:T(8,128)} fusion(f32[8,2,256,384]{3,2,1,0:T(8,128)} %get-tuple-element.28), kind=kLoop, calls=%fused_computation | loop fusion | flops 2359296 | bytes 9437184 | tf_op jit(solution)/shard_map/add | solution.py:45
  46.8 0.0 slice-done
  46.8 0.0 slice-done.1
  46.8 9.4 %multiply_add_fusion.5 = (f32[8,1,256,384]{3,2,1,0:T(8,128)}, f32[8,1,256,384]{3,2,1,0:T(8,128)}, f32[8,1,256,384]{3,2,1,0:T(8,128)}, f32[8,1,256,384]{3,2,1,0:T(8,128)}, f32[8,1,256,384]{3,2,1,0:T(8,128)}) fusion(f32[8,2,256,384]{3,2,1,0:T(8,128)} %get-tuple-element.27, f32[8,2,256,384]{3,2,1,0:T(8,128)S(1)} %bitcast.88, f32[8,2,256,384]{3,2,1,0:T(8,128)} %get-tuple-element.28), kind=kLoop, calls=%fused_computation.8 | loop fusion | flops 11796480 | bytes 34603008 | tf_op jit(solution)/shard_map/add | solution.py:42
  56.1 3.2 %reduce_sum.112 = f32[8,16,384]{2,1,0:T(8,128)} reduce(f32[8,16,16,384]{3,2,1,0:T(8,128)} %bitcast.95, f32[]{:T(128)} %constant.21.clone.1), dimensions={2}, to_apply=%region_3.4 | reduce | flops 737280 | bytes 3342340 | tf_op jit(solution)/shard_map/reduce_sum | solution.py:25
  59.4 1.8 %convolution_multiply_fusion.6 = f32[8,16,96]{2,1,0:T(8,128)} fusion(f32[8,16,384]{2,1,0:T(8,128)} %reduce_sum.112, s32[384]{0:T(512)S(1)} %add_select_fusion), kind=kOutput, calls=%fused_computation.23 | convolution fusion | flops 56672256 | bytes 247296 | tf_op jit(solution)/shard_map/nra,ab->nrb/dot_general | solution.py:26
  61.2 0.0 copy-done.2
  61.2 1.2 reduce_sum.111
  62.3 1.8 %convolution_multiply_fusion.7 = f32[8,16,96]{2,1,0:T(8,128)} fusion(f32[8,16,384]{2,1,0:T(8,128)} %reduce_sum.111, s32[384]{0:T(512)S(1)} %add_select_fusion), kind=kOutput, calls=%fused_computation.24 | convolution fusion | flops 56672256 | bytes 247296 | tf_op jit(solution)/shard_map/nra,ab->nrb/dot_general | solution.py:26
  64.1 3.2 %reduce_sum.117 = f32[8,16,384]{2,1,0:T(8,128)} reduce(f32[8,16,16,384]{3,2,1,0:T(8,128)} %bitcast.92, f32[]{:T(128)} %constant.21.clone.1), dimensions={2}, to_apply=%region_8.9 | reduce | flops 737280 | bytes 3342340 | tf_op jit(solution)/shard_map/reduce_sum | solution.py:25
  67.4 3.1 %reduce_sum.114 = f32[8,16,384]{2,1,0:T(8,128)} reduce(f32[8,16,16,384]{3,2,1,0:T(8,128)} %bitcast.90, f32[]{:T(128)} %constant.21.clone.1), dimensions={2}, to_apply=%region_5.6 | reduce | flops 737280 | bytes 3342340 | tf_op jit(solution)/shard_map/reduce_sum | solution.py:25
  70.4 1.2 convolution_multiply_fusion.4
  71.6 1.2 reduce_sum.113
  72.8 1.2 %convolution_multiply_fusion.5 = f32[8,16,96]{2,1,0:T(8,128)S(1)} fusion(f32[8,16,384]{2,1,0:T(8,128)} %reduce_sum.113, s32[384]{0:T(512)S(1)} %add_select_fusion), kind=kOutput, calls=%fused_computation.22 | convolution fusion | flops 56672256 | bytes 247296 | tf_op jit(solution)/shard_map/nra,ab->nrb/dot_general | solution.py:26
  74.1 2.4 %reduce_sum.118 = f32[8,16,384]{2,1,0:T(8,128)S(1)} reduce(f32[8,16,16,384]{3,2,1,0:T(8,128)} %bitcast.98, f32[]{:T(128)} %constant.21.clone.1), dimensions={2}, to_apply=%region_9.10 | reduce | flops 737280 | bytes 3342340 | tf_op jit(solution)/shard_map/reduce_sum | solution.py:25
  76.5 0.3 fusion.7
  76.8 0.3 fusion.12
  77.1 0.3 fusion.17
  77.4 0.0 copy-start.4
  77.4 0.7 copy-done.4
  78.1 0.4 copy.31
  78.5 0.2 mul.293
  78.6 1.3 %concatenate.10 = f32[24,1,16,16,6]{2,4,3,0,1:T(8,128)} reshape(f32[8,3,16,96]{2,3,1,0:T(8,128)S(1)} %copy.31) | data formatting | bytes 294912 | tf_op jit(solution)/shard_map/concatenate | solution.py:59
  79.9 1.0 copy.32
  80.9 0.9 maximum_bitcast_fusion.4
  81.8 1.0 maximum_bitcast_fusion.2
  82.8 1.2 %copy.33 = f32[8,3,2,16,96]{3,2,4,1,0:T(2,128)S(1)} copy(f32[8,3,2,16,96]{4,3,0,2,1:T(8,128)S(1)} %pad_maximum_fusion) | data formatting | bytes 589824 | tf_op jit(solution)/shard_map/stack | solution.py:51
  84.0 2.9 %copy.34 = f32[24,2,16,16,6]{0,3,4,2,1:T(8,128)} copy(f32[24,2,16,16,6]{2,1,4,3,0:T(2,128)S(1)} %bitcast.100) | data formatting | bytes 589824 | tf_op jit(solution)/shard_map/stack | solution.py:51
  87.0 2.4 %copy.36 = f32[24,1,16,16,6]{0,3,4,2,1:T(8,128)S(1)} copy(f32[24,1,16,16,6]{2,4,3,0,1:T(8,128)} %concatenate.10) | data formatting | bytes 294912 | tf_op jit(solution)/shard_map/concatenate | solution.py:59
  89.3 0.2 broadcast_multiply_fusion
  89.5 0.0 copy-done.13
  89.5 1.3 %fusion = f32[16,24,3,16,6]{1,0,4,3,2:T(8,128)S(1)} fusion(f32[24,1,16,16,6]{0,3,4,2,1:T(8,128)S(1)} %copy.36, f32[24,2,16,16,6]{0,3,4,2,1:T(8,128)S(1)} %broadcast_multiply_fusion, s32[16]{0:T(128)S(1)} %copy-done.13), kind=kOutput, calls=%fused_computation.14 | convolution fusion | flops 21344512 | bytes 884800 | tf_op jit(solution)/shard_map/st,tpcrw->spcrw/dot_general | solution.py:66
  90.8 0.0 copy-start.5
  90.9 1.4 %copy.48 = f32[16,24,3,16,6]{1,3,4,2,0:T(8,128)S(1)} copy(f32[16,24,3,16,6]{1,0,4,3,2:T(8,128)S(1)} %fusion) | data formatting | bytes 884736 | tf_op jit(solution)/shard_map/st,tpcrw->spcrw/dot_general | solution.py:66
  92.2 2.7 %reshape.187 = f32[16,1,6912]{2,1,0:T(1,128)} reshape(f32[16,3,6,16,24]{4,3,2,1,0:T(8,128)S(1)} %bitcast.99) | data formatting | bytes 884736
  94.9 6.0 %all-to-all-start = ((f32[16,1,6912]{2,1,0:T(1,128)}), f32[16,1,6912]{2,1,0:T(1,128)S(1)}, u32[]{:S(2)}, u32[]{:S(2)}) async-start(f32[16,1,6912]{2,1,0:T(1,128)} %reshape.187), calls=%async_computation | async-start | bytes 884736 | tf_op jit(solution)/shard_map/all_to_all | solution.py:67
  100.9 0.7 copy.42
  101.6 0.8 copy.41
  102.4 11.5 %all-to-all-done = f32[16,1,6912]{2,1,0:T(1,128)S(1)} async-done(((f32[16,1,6912]{2,1,0:T(1,128)}), f32[16,1,6912]{2,1,0:T(1,128)S(1)}, u32[]{:S(2)}, u32[]{:S(2)}) %all-to-all-start) | async-done | bytes 442400 | tf_op jit(solution)/shard_map/all_to_all | solution.py:67
  113.8 0.5 broadcast.116
  114.4 1.7 %reduce.3 = f32[16,6912]{1,0:T(8,128)S(1)} reduce(f32[16,1,6912]{2,1,0:T(1,128)S(1)} %all-to-all-done, f32[]{:T(128)} %broadcast.116), dimensions={1}, to_apply=%all_to_all.2.reduce_sub_computation | reduce | bytes 884740 | tf_op jit(solution)/shard_map/all_to_all | solution.py:67
  116.1 1.7 %reshape.188 = f32[16,3,6,16,24]{4,3,2,1,0:T(8,128)S(1)} reshape(f32[16,6912]{1,0:T(8,128)S(1)} %reduce.3) | data formatting | bytes 884736
  117.8 0.2 bitcast_reduce_fusion
  118.0 0.1 copy.46
  118.1 0.7 copy.43
  (27 shorter events, 0.1 us)
Async XLA Ops:
  2.0 19.2 %collective-permute-start = (bf16[3,2,256,384]{3,2,1,0:T(8,128)(2,1)S(1)}, bf16[3,2,256,384]{3,2,1,0:T(8,128)(2,1)S(1)}, u32[]{:S(2)}, u32[]{:S(2)}) collective-permute-start(bf16[3,2,256,384]{3,2,1,0:T(8,128)(2,1)S(1)} %slice.36), channel_id=1, source_target_pairs={{0,30},{2,0},{4,2},{6,4},{8,6},{10,8},{12,10},{14,12},{16,14},{18,... | collective-permute-start | bytes 3538952 | tf_op jit(solution)/shard_map/ppermute | solution.py:14
  12.0 14.9 %copy-start = (f32[8,2,256,384]{3,2,1,0:T(8,128)}, f32[8,2,256,384]{3,2,1,0:T(8,128)S(1)}, u32[]{:S(2)}) copy-start(f32[8,2,256,384]{3,2,1,0:T(8,128)S(1)} %get-tuple-element.29) | copy-start | bytes 18874372
  37.8 38.7 %copy-start.9 = (f32[8,16,96]{2,1,0:T(8,128)}, f32[8,16,96]{2,1,0:T(8,128)S(1)}, u32[]{:S(2)}) copy-start(f32[8,16,96]{2,1,0:T(8,128)S(1)} %convolution_multiply_fusion.8) | copy-start | bytes 147460
  39.2 7.6 %slice-start = ((s8[6291456]{0:T(1024)(128)(4,1)}), s8[2097152]{0:T(1024)(128)(4,1)S(1)}, s32[]{:S(2)}) async-start(s8[6291456]{0:T(1024)(128)(4,1)} %bitcast.87), calls=%async_computation.1 | async-start | bytes 4194304
  41.7 5.0 %slice-start.1 = ((s8[6291456]{0:T(1024)(128)(4,1)}), s8[4194304]{0:T(1024)(128)(4,1)S(1)}, s32[]{:S(2)}) async-start(s8[6291456]{0:T(1024)(128)(4,1)} %bitcast.87), calls=%async_computation.2 | async-start | bytes 8388608
  56.1 5.0 %copy-start.2 = (f32[8,1,256,384]{3,2,1,0:T(8,128)S(1)}, f32[8,1,256,384]{3,2,1,0:T(8,128)}, u32[]{:S(2)}) copy-start(f32[8,1,256,384]{3,2,1,0:T(8,128)} %get-tuple-element.17) | copy-start | bytes 9437188
  64.1 7.5 %copy-start.1 = (f32[8,1,256,384]{3,2,1,0:T(8,128)S(1)}, f32[8,1,256,384]{3,2,1,0:T(8,128)}, u32[]{:S(2)}) copy-start(f32[8,1,256,384]{3,2,1,0:T(8,128)} %get-tuple-element.25) | copy-start | bytes 9437188
  71.6 5.5 %copy-start.7 = (f32[8,16,96]{2,1,0:T(8,128)}, f32[8,16,96]{2,1,0:T(8,128)S(1)}, u32[]{:S(2)}) copy-start(f32[8,16,96]{2,1,0:T(8,128)S(1)} %convolution_multiply_fusion.4) | copy-start | bytes 147460
  72.8 3.7 %copy-start.10 = (f32[8,16,96]{2,1,0:T(8,128)S(1)}, f32[8,16,96]{2,1,0:T(8,128)}, u32[]{:S(2)}) copy-start(f32[8,16,96]{2,1,0:T(8,128)} %convolution_multiply_fusion.9) | copy-start | bytes 147460
  72.8 4.0 %copy-start.6 = (f32[8,16,384]{2,1,0:T(8,128)S(1)}, f32[8,16,384]{2,1,0:T(8,128)}, u32[]{:S(2)}) copy-start(f32[8,16,384]{2,1,0:T(8,128)} %reduce_sum.117) | copy-start | bytes 589828
  72.8 4.0 %copy-start.11 = (f32[8,16,96]{2,1,0:T(8,128)S(1)}, f32[8,16,96]{2,1,0:T(8,128)}, u32[]{:S(2)}) copy-start(f32[8,16,96]{2,1,0:T(8,128)} %convolution_multiply_fusion.6) | copy-start | bytes 147460
  72.8 4.0 %copy-start.12 = (f32[8,16,96]{2,1,0:T(8,128)S(1)}, f32[8,16,96]{2,1,0:T(8,128)}, u32[]{:S(2)}) copy-start(f32[8,16,96]{2,1,0:T(8,128)} %convolution_multiply_fusion.7) | copy-start | bytes 147460
  74.1 3.3 %copy-start.8 = (f32[8,16,96]{2,1,0:T(8,128)}, f32[8,16,96]{2,1,0:T(8,128)S(1)}, u32[]{:S(2)}) copy-start(f32[8,16,96]{2,1,0:T(8,128)S(1)} %convolution_multiply_fusion.5) | copy-start | bytes 147460
  77.4 0.7 copy-start.4
  87.0 2.4 %copy-start.3 = (f32[24,2,16,16,6]{0,3,4,2,1:T(8,128)S(1)}, f32[24,2,16,16,6]{0,3,4,2,1:T(8,128)}, u32[]{:S(2)}) copy-start(f32[24,2,16,16,6]{0,3,4,2,1:T(8,128)} %copy.34) | copy-start | bytes 884740
  87.0 2.5 %copy-start.13 = (s32[16]{0:T(128)S(1)}, s32[16]{0:T(128)}, u32[]{:S(2)}) copy-start(s32[16]{0:T(128)} %param.5) | copy-start | bytes 196
  90.8 10.1 %copy-start.5 = (f32[8,3,16,96]{3,2,0,1:T(8,128)S(1)}, f32[8,3,16,96]{3,2,0,1:T(8,128)}, u32[]{:S(2)}) copy-start(f32[8,3,16,96]{3,2,0,1:T(8,128)} %copy-done.4) | copy-start | bytes 442372
  94.9 18.9 %all-to-all-start = ((f32[16,1,6912]{2,1,0:T(1,128)}), f32[16,1,6912]{2,1,0:T(1,128)S(1)}, u32[]{:S(2)}, u32[]{:S(2)}) async-start(f32[16,1,6912]{2,1,0:T(1,128)} %reshape.187), calls=%async_computation | async-start | bytes 884736 | tf_op jit(solution)/shard_map/all_to_all | solution.py:67
where the time goes:
time: 119 us
  other arithmetic  55.1 us (46%)
  waiting for transfers between devices  20.6 us (17%)
  local copies, waits for them, and re-layouts  20.2 us (17%)
  starting transfers between devices  11.5 us (10%)
  matrix products  10.4 us (9%)
    reduce_sum x10, other arithmetic, looks(): ranged = field.reshape(count, rows // LR, LR, cols).sum(2)  22.8 us
    add x2, other arithmetic, pair_block(): real_part = looks(own[:, 0] * other[:, 0] + own[:, 1] * other[:, 1], pool)  13.3 us
    all_to_all x1, waiting for transfers between devices, on_device(): lax.all_to_all(slotted, 'date', split_axis=0, concat_axis=1, tiled=True)  11.5 us
    ppermute x1, waiting for transfers between devices, shifted(): return lax.ppermute(value, axis, pairs)  9.19 us
    dot_general x10, matrix products, looks(): jnp.einsum('nra,ab->nrb', ranged, pool, precision=lax.Precision.HIGHEST)  9.11 us
    unnamed x38, local copies, waits for them, and re-layouts  7.37 us
    all_to_all x1, starting transfers between devices, on_device(): lax.all_to_all(slotted, 'date', split_axis=0, concat_axis=1, tiled=True)  5.98 us
    ppermute x1, starting transfers between devices, shifted(): return lax.ppermute(value, axis, pairs)  5.5 us
  transfers between devices with their start and end apart: 2, of which 2 were waited for; matrix products, arithmetic and copies ran while one was open for 5% of the time, Pallas kernels for 0%

commit v1 on v0

--- a/solution.py
+++ b/solution.py
@@ -64,7 +64,10 @@
     onehot = (owner[None, :] == slots[:, None]).astype(jnp.float32)
     flat = weighted.reshape(count * NB, 3, rows_loc, tile_count, width).transpose(3, 0, 1, 2, 4)
     slotted = jnp.einsum("st,tpcrw->spcrw", onehot, flat, precision=lax.Precision.HIGHEST)
-    sums = lax.all_to_all(slotted, "date", split_axis=0, concat_axis=1, tiled=True).sum(1)
+    sums = jnp.concatenate(
+        lax.all_to_all(jnp.stack(jnp.split(slotted, lax.axis_size("date"), axis=0)), "date", 0, 0),
+        axis=1,
+    ).sum(1)
     network_mean = sums[:, :2] / (1.0 + sums[:, 2:3])
     return (interferograms, coherence, network_mean)
 

time: 119 us -> 130 us (1.092)
  local copies, waits for them, and re-layouts: 20.2 us -> 32.7 us
    another operation x0 -> x3, local copies, waits for them, and re-layouts: none -> 11.3 us  [on_device(): jnp.stack(jnp.split(slotted, lax.axis_size('date'), axis=0))]
    another operation x4, other arithmetic: 1.89 us -> 0.08 us  [pair_block(): return (jnp.stack(pairs, 1), jnp.stack(coher, 1))]
    unnamed x38 -> x31, local copies, waits for them, and re-layouts: 7.37 us -> 9.11 us
    dot_general x1 -> x0, local copies, waits for them, and re-layouts: 1.37 us -> none  [on_device(): jnp.einsum('st,tpcrw->spcrw', onehot, flat, precision=lax.Precision.HIGHEST)]
where the time goes in v1:
time: 130 us; the launch traced here: 129 us
  other arithmetic  54.2 us (42%)
  local copies, waits for them, and re-layouts  32.7 us (25%)
  waiting for transfers between devices  19.7 us (15%)
  starting transfers between devices  11.5 us (9%)
  matrix products  10.4 us (8%)
    reduce_sum x10, other arithmetic, looks(): ranged = field.reshape(count, rows // LR, LR, cols).sum(2)  22.8 us
    add x2, other arithmetic, pair_block(): real_part = looks(own[:, 0] * other[:, 0] + own[:, 1] * other[:, 1], pool)  13.3 us
    another operation x3, local copies, waits for them, and re-layouts, on_device(): jnp.stack(jnp.split(slotted, lax.axis_size('date'), axis=0))  11.3 us
    all_to_all x1, waiting for transfers between devices, on_device(): lax.all_to_all(jnp.stack(jnp.split(slotted, lax.axis_size('date'), axis=0...  10.5 us
    ppermute x1, waiting for transfers between devices, shifted(): return lax.ppermute(value, axis, pairs)  9.19 us
    dot_general x10, matrix products, looks(): jnp.einsum('nra,ab->nrb', ranged, pool, precision=lax.Precision.HIGHEST)  9.12 us
    unnamed x31, local copies, waits for them, and re-layouts  9.11 us
    all_to_all x1, starting transfers between devices, on_device(): lax.all_to_all(jnp.stack(jnp.split(slotted, lax.axis_size('date'), axis=0...  5.98 us
  transfers between devices with their start and end apart: 2, of which 2 were waited for; matrix products, arithmetic and copies ran while one was open for 5% of the time, Pallas kernels for 0%

profile of v1, /device:TPU:0, one launch (start us, length us, event | category | flops | bytes accessed | tf_op | source)
XLA Modules:
  0.0 129.4 jit_solution(5605930230837933629)
XLA Ops:
  0.6 1.4 %slice.36 = bf16[3,2,256,384]{3,2,1,0:T(8,128)(2,1)S(1)} slice(bf16[8,2,256,384]{3,2,1,0:T(8,128)(2,1)} %param.3), slice={[0:3], [0:2], [0:256], [0:384]} | slice | bytes 2359296 | tf_op jit(solution)/shard_map/slice | solution.py:56
  2.0 5.5 %collective-permute-start = (bf16[3,2,256,384]{3,2,1,0:T(8,128)(2,1)S(1)}, bf16[3,2,256,384]{3,2,1,0:T(8,128)(2,1)S(1)}, u32[]{:S(2)}, u32[]{:S(2)}) collective-permute-start(bf16[3,2,256,384]{3,2,1,0:T(8,128)(2,1)S(1)} %slice.36), channel_id=1, source_target_pairs={{0,30},{2,0},{4,2},{6,4},{8,6},{10,8},{12,10},{14,12},{16,14},{18,... | collective-permute-start | bytes 3538952 | tf_op jit(solution)/shard_map/ppermute | solution.py:14
  7.5 0.8 compare_bitcast_fusion.5
  8.3 3.7 %fusion.47 = (f32[8,2,256,384]{3,2,1,0:T(8,128)S(1)}, bf16[11,2,256,384]{3,2,1,0:T(8,128)(2,1)S(1)}) fusion(bf16[8,2,256,384]{3,2,1,0:T(8,128)(2,1)} %param.3), kind=kLoop, calls=%fused_computation.98 | loop fusion | flops 1572863 | bytes 12582912 | tf_op jit(solution)/shard_map/convert_element_type | solution.py:32
  12.0 0.0 copy-start
  12.1 9.2 %collective-permute-done = bf16[3,2,256,384]{3,2,1,0:T(8,128)(2,1)S(1)} collective-permute-done((bf16[3,2,256,384]{3,2,1,0:T(8,128)(2,1)S(1)}, bf16[3,2,256,384]{3,2,1,0:T(8,128)(2,1)S(1)}, u32[]{:S(2)}, u32[]{:S(2)}) %collective-permute-start) | collective-permute-done | bytes 1179680 | tf_op jit(solution)/shard_map/ppermute | solution.py:14
  21.2 0.2 constant_dynamic-update-slice_fusion
  21.5 5.4 %select_convert_fusion.2 = (f32[8,2,256,384]{3,2,1,0:T(8,128)S(1)}, f32[8,2,256,384]{3,2,1,0:T(8,128)}, f32[8,2,256,384]{3,2,1,0:T(8,128)}) fusion(pred[8]{0:T(512)(128)(4,1)S(1)} %get-tuple-element.45, pred[8]{0:T(512)(128)(4,1)S(1)} %get-tuple-element.44, bf16[11,2,256,384]{3,2,1,0:T(8,128)(2,1)S(1)} %constant_dynamic-update-slice_fusion, ...), kind=kLoop, calls=%fused_computation.12 | loop fusion | flops 14155776 | bytes 28311600 | tf_op jit(solution)/shard_map/convert_element_type | solution.py:41
  26.9 0.0 copy-done
  26.9 4.0 %multiply_add_fusion.6 = (f32[8,1,256,384]{3,2,1,0:T(8,128)S(1)}, f32[8,1,256,384]{3,2,1,0:T(8,128)}, f32[8,1,256,384]{3,2,1,0:T(8,128)}, f32[8,1,256,384]{3,2,1,0:T(8,128)}) fusion(f32[8,2,256,384]{3,2,1,0:T(8,128)S(1)} %get-tuple-element.23, f32[8,2,256,384]{3,2,1,0:T(8,128)S(1)} %get-tuple-element.26), kind=kLoop, calls=%fused_computation.11 | loop fusion | flops 9437184 | bytes 25165824 | tf_op jit(solution)/shard_map/add | solution.py:42
  30.9 2.4 %reduce_sum.115 = f32[8,16,384]{2,1,0:T(8,128)S(1)} reduce(f32[8,16,16,384]{3,2,1,0:T(8,128)} %bitcast.129, f32[]{:T(128)} %constant.21.clone.1), dimensions={2}, to_apply=%region_6.7 | reduce | flops 737280 | bytes 3342340 | tf_op jit(solution)/shard_map/reduce_sum | solution.py:25
  33.3 3.1 %reduce_sum.110 = f32[8,16,384]{2,1,0:T(8,128)} reduce(f32[8,16,16,384]{3,2,1,0:T(8,128)} %bitcast.128, f32[]{:T(128)} %constant.21.clone.1), dimensions={2}, to_apply=%region_1.2 | reduce | flops 737280 | bytes 3342340 | tf_op jit(solution)/shard_map/reduce_sum | solution.py:25
  36.3 0.3 convolution_multiply_fusion.3
  36.6 1.2 convolution_multiply_fusion.8
  37.8 0.5 reduce_sum.109
  38.3 0.9 convolution_multiply_fusion.9
  39.2 2.5 %reduce_sum.116 = f32[8,16,384]{2,1,0:T(8,128)S(1)} reduce(f32[8,16,16,384]{3,2,1,0:T(8,128)} %bitcast.123, f32[]{:T(128)} %constant.21.clone.1), dimensions={2}, to_apply=%region_7.8 | reduce | flops 737280 | bytes 3342340 | tf_op jit(solution)/shard_map/reduce_sum | solution.py:25
  41.7 0.0 slice-start.1
  41.7 5.0 %multiply_add_fusion = f32[8,1,256,384]{3,2,1,0:T(8,128)} fusion(f32[8,2,256,384]{3,2,1,0:T(8,128)} %get-tuple-element.25), kind=kLoop, calls=%fused_computation | loop fusion | flops 2359296 | bytes 9437184 | tf_op jit(solution)/shard_map/add | solution.py:45
  46.8 0.0 slice-done
  46.8 0.0 slice-done.1
  46.8 9.4 %multiply_add_fusion.5 = (f32[8,1,256,384]{3,2,1,0:T(8,128)}, f32[8,1,256,384]{3,2,1,0:T(8,128)}, f32[8,1,256,384]{3,2,1,0:T(8,128)}, f32[8,1,256,384]{3,2,1,0:T(8,128)}, f32[8,1,256,384]{3,2,1,0:T(8,128)}) fusion(f32[8,2,256,384]{3,2,1,0:T(8,128)} %get-tuple-element.24, f32[8,2,256,384]{3,2,1,0:T(8,128)S(1)} %bitcast.120, ...), kind=kLoop, calls=%fused_computation.8 | loop fusion | flops 11796480 | bytes 34603008 | tf_op jit(solution)/shard_map/add | solution.py:42
  56.1 3.2 %reduce_sum.112 = f32[8,16,384]{2,1,0:T(8,128)} reduce(f32[8,16,16,384]{3,2,1,0:T(8,128)} %bitcast.127, f32[]{:T(128)} %constant.21.clone.1), dimensions={2}, to_apply=%region_3.4 | reduce | flops 737280 | bytes 3342340 | tf_op jit(solution)/shard_map/reduce_sum | solution.py:25
  59.4 1.8 %convolution_multiply_fusion.6 = f32[8,16,96]{2,1,0:T(8,128)} fusion(f32[8,16,384]{2,1,0:T(8,128)} %reduce_sum.112, s32[384]{0:T(512)S(1)} %add_select_fusion), kind=kOutput, calls=%fused_computation.23 | convolution fusion | flops 56672256 | bytes 247296 | tf_op jit(solution)/shard_map/nra,ab->nrb/dot_general | solution.py:26
  61.2 0.0 copy-done.2
  61.2 1.2 reduce_sum.111
  62.3 1.8 %convolution_multiply_fusion.7 = f32[8,16,96]{2,1,0:T(8,128)} fusion(f32[8,16,384]{2,1,0:T(8,128)} %reduce_sum.111, s32[384]{0:T(512)S(1)} %add_select_fusion), kind=kOutput, calls=%fused_computation.24 | convolution fusion | flops 56672256 | bytes 247296 | tf_op jit(solution)/shard_map/nra,ab->nrb/dot_general | solution.py:26
  64.1 3.2 %reduce_sum.117 = f32[8,16,384]{2,1,0:T(8,128)} reduce(f32[8,16,16,384]{3,2,1,0:T(8,128)} %bitcast.124, f32[]{:T(128)} %constant.21.clone.1), dimensions={2}, to_apply=%region_8.9 | reduce | flops 737280 | bytes 3342340 | tf_op jit(solution)/shard_map/reduce_sum | solution.py:25
  67.4 3.1 %reduce_sum.114 = f32[8,16,384]{2,1,0:T(8,128)} reduce(f32[8,16,16,384]{3,2,1,0:T(8,128)} %bitcast.122, f32[]{:T(128)} %constant.21.clone.1), dimensions={2}, to_apply=%region_5.6 | reduce | flops 737280 | bytes 3342340 | tf_op jit(solution)/shard_map/reduce_sum | solution.py:25
  70.4 1.2 convolution_multiply_fusion.4
  71.6 0.0 copy-done.1
  71.6 1.2 reduce_sum.113
  72.8 1.2 convolution_multiply_fusion.5
  74.0 2.4 %reduce_sum.118 = f32[8,16,384]{2,1,0:T(8,128)S(1)} reduce(f32[8,16,16,384]{3,2,1,0:T(8,128)} %bitcast.131, f32[]{:T(128)} %constant.21.clone.1), dimensions={2}, to_apply=%region_9.10 | reduce | flops 737280 | bytes 3342340 | tf_op jit(solution)/shard_map/reduce_sum | solution.py:25
  76.4 0.0 copy-done.7
  76.5 0.3 fusion.7
  76.7 0.0 copy-done.6
  76.7 0.0 copy-done.8
  76.8 0.3 fusion.12
  77.0 0.3 fusion.17
  77.3 0.0 copy-start.5
  77.3 0.7 copy-done.5
  78.0 0.4 copy.18
  78.4 0.2 mul.293
  78.5 1.3 %concatenate.10 = f32[24,1,16,16,6]{2,4,3,0,1:T(8,128)} reshape(f32[8,3,16,96]{2,3,1,0:T(8,128)S(1)} %copy.18) | data formatting | bytes 294912 | tf_op jit(solution)/shard_map/concatenate | solution.py:59
  79.8 1.9 %copy.19 = f32[24,16,16,6]{0,2,3,1:T(8,128)} copy(f32[24,16,16,6]{1,3,2,0:T(8,128)S(1)} %mul.293) | data formatting | bytes 294912 | tf_op jit(solution)/shard_map/mul | solution.py:59
  81.8 1.2 copy.20
  83.0 2.9 %copy.21 = f32[24,2,16,16,6]{0,3,4,2,1:T(8,128)} copy(f32[24,2,16,16,6]{2,1,4,3,0:T(2,128)S(1)} %bitcast.132) | data formatting | bytes 589824 | tf_op jit(solution)/shard_map/stack | solution.py:51
  85.9 2.4 %copy.23 = f32[24,1,16,16,6]{0,3,4,2,1:T(8,128)S(1)} copy(f32[24,1,16,16,6]{2,4,3,0,1:T(8,128)} %concatenate.10) | data formatting | bytes 294912 | tf_op jit(solution)/shard_map/concatenate | solution.py:59
  88.3 0.2 broadcast_multiply_fusion
  88.5 1.3 %fusion = f32[16,24,3,16,6]{1,0,4,3,2:T(8,128)S(1)} fusion(f32[24,1,16,16,6]{0,3,4,2,1:T(8,128)S(1)} %copy.23, f32[24,2,16,16,6]{0,3,4,2,1:T(8,128)S(1)} %broadcast_multiply_fusion, s32[16]{0:T(128)S(1)} %copy-done.10), kind=kOutput, calls=%fused_computation.14 | convolution fusion | flops 21344512 | bytes 884800 | tf_op jit(solution)/shard_map/st,tpcrw->spcrw/dot_general | solution.py:66
  89.8 2.3 %slice_bitcast_fusion = (f32[1,1,24,3,16,6]{2,0,5,4,3,1:T(1,128)S(1)}, f32[1,1,24,3,16,6]{2,0,5,4,3,1:T(1,128)S(1)}, f32[1,1,24,3,16,6]{2,0,5,4,3,1:T(1,128)S(1)...) fusion(f32[16,24,3,16,6]{1,0,4,3,2:T(8,128)S(1)} %fusion), kind=kLoop, calls=%fused_computation.45 | loop fusion | bytes 884736 | tf_op jit(solution)/shard_map/stack | solution.py:68
  92.2 6.5 %stack.138 = f32[16,1,24,3,16,6]{2,0,5,4,3,1:T(8,128)} concatenate(f32[1,1,24,3,16,6]{2,0,5,4,3,1:T(1,128)S(1)} %get-tuple-element.43, f32[1,1,24,3,16,6]{2,0,5,4,3,1:T(1,128)S(1)} %get-tuple-element.42, f32[1,1,24,3,16,6]{2,0,5,4,3,1:T(1,128)S(1)} %get-tuple-element.41, f32[1,1,24,3,16,6]{2,0,5,4,3,1:T(1,128)S(1)} %get-tuple-element.40, ...), dimensions={0} | concatenate | bytes 884736 | tf_op jit(solution)/shard_map/stack | solution.py:68
  98.7 2.5 %copy.35 = f32[16,1,24,3,16,6]{2,5,4,3,1,0:T(8,128)S(1)} copy(f32[16,1,24,3,16,6]{2,0,5,4,3,1:T(8,128)} %stack.138) | data formatting | bytes 884736 | tf_op jit(solution)/shard_map/stack | solution.py:68
  101.1 2.6 %reshape.186 = f32[16,1,6912]{2,1,0:T(1,128)} reshape(f32[16,1,3,16,6,24]{5,4,3,2,1,0:T(8,128)S(1)} %bitcast.130) | data formatting | bytes 884736
  103.7 6.0 %all-to-all-start = ((f32[16,1,6912]{2,1,0:T(1,128)}), f32[16,1,6912]{2,1,0:T(1,128)S(1)}, u32[]{:S(2)}, u32[]{:S(2)}) async-start(f32[16,1,6912]{2,1,0:T(1,128)} %reshape.186), calls=%async_computation | async-start | bytes 884736 | tf_op jit(solution)/shard_map/all_to_all | solution.py:68
  109.7 1.6 %copy.29 = f32[8,3,16,96]{3,2,1,0:T(8,128)} copy(f32[8,3,16,96]{3,2,0,1:T(8,128)} %copy-done.5) | data formatting | bytes 294912
  111.3 0.8 copy.28
  112.1 10.5 %all-to-all-done = f32[16,1,6912]{2,1,0:T(1,128)S(1)} async-done(((f32[16,1,6912]{2,1,0:T(1,128)}), f32[16,1,6912]{2,1,0:T(1,128)S(1)}, u32[]{:S(2)}, u32[]{:S(2)}) %all-to-all-start) | async-done | bytes 442400 | tf_op jit(solution)/shard_map/all_to_all | solution.py:68
  122.7 0.5 broadcast.116
  123.2 2.5 %reduce.2 = f32[16,6912]{1,0:T(8,128)} reduce(f32[16,1,6912]{2,1,0:T(1,128)S(1)} %all-to-all-done, f32[]{:T(128)} %broadcast.116), dimensions={1}, to_apply=%all_to_all.3.reduce_sub_computation | reduce | bytes 884740 | tf_op jit(solution)/shard_map/all_to_all | solution.py:68
  125.7 2.7 %reshape.187 = f32[16,1,3,16,6,24]{5,4,3,2,1,0:T(8,128)S(1)} reshape(f32[16,6912]{1,0:T(8,128)} %reduce.2) | data formatting | bytes 884736
  128.4 0.3 bitcast_reduce_fusion
  128.8 0.7 copy.30
  (22 shorter events, 0.1 us)
Async XLA Ops:
  2.0 19.2 %collective-permute-start = (bf16[3,2,256,384]{3,2,1,0:T(8,128)(2,1)S(1)}, bf16[3,2,256,384]{3,2,1,0:T(8,128)(2,1)S(1)}, u32[]{:S(2)}, u32[]{:S(2)}) collective-permute-start(bf16[3,2,256,384]{3,2,1,0:T(8,128)(2,1)S(1)} %slice.36), channel_id=1, source_target_pairs={{0,30},{2,0},{4,2},{6,4},{8,6},{10,8},{12,10},{14,12},{16,14},{18,... | collective-permute-start | bytes 3538952 | tf_op jit(solution)/shard_map/ppermute | solution.py:14
  12.0 14.9 %copy-start = (f32[8,2,256,384]{3,2,1,0:T(8,128)}, f32[8,2,256,384]{3,2,1,0:T(8,128)S(1)}, u32[]{:S(2)}) copy-start(f32[8,2,256,384]{3,2,1,0:T(8,128)S(1)} %get-tuple-element.26) | copy-start | bytes 18874372
  39.2 7.6 %slice-start = ((s8[6291456]{0:T(1024)(128)(4,1)}), s8[2097152]{0:T(1024)(128)(4,1)S(1)}, s32[]{:S(2)}) async-start(s8[6291456]{0:T(1024)(128)(4,1)} %bitcast.119), calls=%async_computation.1 | async-start | bytes 4194304
  41.7 5.0 %slice-start.1 = ((s8[6291456]{0:T(1024)(128)(4,1)}), s8[4194304]{0:T(1024)(128)(4,1)S(1)}, s32[]{:S(2)}) async-start(s8[6291456]{0:T(1024)(128)(4,1)} %bitcast.119), calls=%async_computation.2 | async-start | bytes 8388608
  56.1 5.0 %copy-start.2 = (f32[8,1,256,384]{3,2,1,0:T(8,128)S(1)}, f32[8,1,256,384]{3,2,1,0:T(8,128)}, u32[]{:S(2)}) copy-start(f32[8,1,256,384]{3,2,1,0:T(8,128)} %get-tuple-element.14) | copy-start | bytes 9437188
  64.1 7.5 %copy-start.1 = (f32[8,1,256,384]{3,2,1,0:T(8,128)S(1)}, f32[8,1,256,384]{3,2,1,0:T(8,128)}, u32[]{:S(2)}) copy-start(f32[8,1,256,384]{3,2,1,0:T(8,128)} %get-tuple-element.22) | copy-start | bytes 9437188
  72.8 3.6 %copy-start.7 = (f32[8,16,96]{2,1,0:T(8,128)S(1)}, f32[8,16,96]{2,1,0:T(8,128)}, u32[]{:S(2)}) copy-start(f32[8,16,96]{2,1,0:T(8,128)} %convolution_multiply_fusion.9) | copy-start | bytes 147460
  72.8 3.9 %copy-start.6 = (f32[8,16,384]{2,1,0:T(8,128)S(1)}, f32[8,16,384]{2,1,0:T(8,128)}, u32[]{:S(2)}) copy-start(f32[8,16,384]{2,1,0:T(8,128)} %reduce_sum.117) | copy-start | bytes 589828
  72.8 3.9 %copy-start.8 = (f32[8,16,96]{2,1,0:T(8,128)S(1)}, f32[8,16,96]{2,1,0:T(8,128)}, u32[]{:S(2)}) copy-start(f32[8,16,96]{2,1,0:T(8,128)} %convolution_multiply_fusion.6) | copy-start | bytes 147460
  72.8 3.9 %copy-start.9 = (f32[8,16,96]{2,1,0:T(8,128)S(1)}, f32[8,16,96]{2,1,0:T(8,128)}, u32[]{:S(2)}) copy-start(f32[8,16,96]{2,1,0:T(8,128)} %convolution_multiply_fusion.7) | copy-start | bytes 147460
  77.3 0.7 copy-start.5
  83.0 5.3 %copy-start.4 = (f32[24,16,16,6]{0,2,3,1:T(8,128)S(1)}, f32[24,16,16,6]{0,2,3,1:T(8,128)}, u32[]{:S(2)}) copy-start(f32[24,16,16,6]{0,2,3,1:T(8,128)} %copy.19) | copy-start | bytes 442372
  85.9 2.4 %copy-start.3 = (f32[24,2,16,16,6]{0,3,4,2,1:T(8,128)S(1)}, f32[24,2,16,16,6]{0,3,4,2,1:T(8,128)}, u32[]{:S(2)}) copy-start(f32[24,2,16,16,6]{0,3,4,2,1:T(8,128)} %copy.21) | copy-start | bytes 884740
  85.9 2.6 %copy-start.10 = (s32[16]{0:T(128)S(1)}, s32[16]{0:T(128)}, u32[]{:S(2)}) copy-start(s32[16]{0:T(128)} %param.5) | copy-start | bytes 196
  103.7 18.9 %all-to-all-start = ((f32[16,1,6912]{2,1,0:T(1,128)}), f32[16,1,6912]{2,1,0:T(1,128)S(1)}, u32[]{:S(2)}, u32[]{:S(2)}) async-start(f32[16,1,6912]{2,1,0:T(1,128)} %reshape.186), calls=%async_computation | async-start | bytes 884736 | tf_op jit(solution)/shard_map/all_to_all | solution.py:68
